TPU v7x, 32 devices: a whole 2x2x4 slice. The times are simulated.
32 devices in a mesh: region: 2 (over y), tile: 4 (over z), corner: 2 (over x), kern: 2 (over core).
Axes of the slice: x: 2, y: 2, z: 4, core: 2. Of those that a mesh axis runs over, the one named last changes fastest.
Arguments:
- tile_mask: bfloat16 [16, 256, 256], P(('region', 'tile')), parts along dimension 0, may hold values from -1 to 1
- master_mask: bfloat16 [8, 256, 256], P(('region', 'tile')), parts along dimension 0, may hold values from -1 to 1
- target: bfloat16 [16, 256, 256], P(('region', 'tile')), parts along dimension 0, may hold values from 0 to 1
- inst_master: int32 [16], P(('region', 'tile')), parts along dimension 0, may hold values from 0 to 3, as said below
- inst_shift: int32 [16, 2], P(('region', 'tile')), parts along dimension 0, may hold values from 0 to 255
- kernels: float32 [2, 12, 2, 32, 32], P('corner'), may hold values from -24 to 24
- kernel_weight: float32 [2, 12], P('corner'), may hold values from 0.05 to 1
- corner_dose: float32 [2], P('corner'), may hold values from 0.6 to 1.6
Outputs:
- tile_grad: float32 [16, 256, 256], P(('region', 'tile')), parts along dimension 0
- master_grad: float32 [8, 256, 256], P(('region', 'tile')), parts along dimension 0
There are 2 independent parts, one for each index of `region`. A program takes and returns all parts, laid end to end along the dimension named above; an argument that names none is the same for every part. Nothing has to cross between parts.
Inputs may be any that keep to these rules, and one draw needn't show every extreme that they name: `inst_master`: each master cell is placed in exactly 2 tiles.
All inputs are finite; a program needn't handle non-finite values.
Results may differ from a plain program's by a relative error of at most 0.0003.
Values may be sent and summed in bfloat16 or wider, within the bound.
No kernel may reach another device: no remote copies, remote signals or barrier semaphores. Data moves between devices by JAX's collectives and lax.ppermute only.
A program may use at most 64 MiB of HBM per device.

v0:
```python
import math
import jax
import jax.numpy as jnp
from jax import lax
from jax.sharding import PartitionSpec as P

P_SIZE = 256
B = 32
precise = lax.Precision.HIGHEST
steepness = 3.0
threshold = 1.0


def band_tables():
    freq = jnp.arange(B, dtype=jnp.int32) - B // 2
    pixel = jnp.arange(P_SIZE, dtype=jnp.int32)
    angle = (
        2.0 * math.pi / P_SIZE * jnp.mod(freq[:, None] * pixel[None, :], P_SIZE).astype(jnp.float32)
    )
    return (jnp.cos(angle), -jnp.sin(angle))


def phase_ramp(shift):
    freq = jnp.arange(B, dtype=jnp.int32) - B // 2
    total = (
        freq[None, :, None] * shift[:, 0][:, None, None]
        + freq[None, None, :] * shift[:, 1][:, None, None]
    )
    angle = 2.0 * math.pi / P_SIZE * jnp.mod(total, P_SIZE).astype(jnp.float32)
    return (jnp.cos(angle), -jnp.sin(angle))


def spectra(masks, cos_tab, sin_tab):
    rows_re = jnp.einsum("bx,nxy->nby", cos_tab, masks, precision=precise)
    rows_im = jnp.einsum("bx,nxy->nby", sin_tab, masks, precision=precise)
    spec_re = jnp.einsum("nby,cy->nbc", rows_re, cos_tab, precision=precise) - jnp.einsum(
        "nby,cy->nbc", rows_im, sin_tab, precision=precise
    )
    spec_im = jnp.einsum("nby,cy->nbc", rows_re, sin_tab, precision=precise) + jnp.einsum(
        "nby,cy->nbc", rows_im, cos_tab, precision=precise
    )
    return (spec_re, spec_im)


def to_field(x_re, x_im, cos_tab, sin_tab, scale):
    half_re = jnp.einsum("bx,nbc->nxc", cos_tab, x_re, precision=precise) + jnp.einsum(
        "bx,nbc->nxc", sin_tab, x_im, precision=precise
    )
    half_im = jnp.einsum("bx,nbc->nxc", cos_tab, x_im, precision=precise) - jnp.einsum(
        "bx,nbc->nxc", sin_tab, x_re, precision=precise
    )
    out_re = (
        jnp.einsum("nxc,cy->nxy", half_re, cos_tab, precision=precise)
        + jnp.einsum("nxc,cy->nxy", half_im, sin_tab, precision=precise)
    ) * scale
    out_im = (
        jnp.einsum("nxc,cy->nxy", half_im, cos_tab, precision=precise)
        - jnp.einsum("nxc,cy->nxy", half_re, sin_tab, precision=precise)
    ) * scale
    return (out_re, out_im)


def back_pixels(x_re, x_im, cos_tab, sin_tab):
    half_re = jnp.einsum("bx,nbc->nxc", cos_tab, x_re, precision=precise) + jnp.einsum(
        "bx,nbc->nxc", sin_tab, x_im, precision=precise
    )
    half_im = jnp.einsum("bx,nbc->nxc", cos_tab, x_im, precision=precise) - jnp.einsum(
        "bx,nbc->nxc", sin_tab, x_re, precision=precise
    )
    return jnp.einsum("nxc,cy->nxy", half_re, cos_tab, precision=precise) + jnp.einsum(
        "nxc,cy->nxy", half_im, sin_tab, precision=precise
    )


def adjoint(g_re, g_im, cos_tab, sin_tab, scale):
    mid_re = jnp.einsum("bx,nxy->nby", cos_tab, g_re, precision=precise) - jnp.einsum(
        "bx,nxy->nby", sin_tab, g_im, precision=precise
    )
    mid_im = jnp.einsum("bx,nxy->nby", cos_tab, g_im, precision=precise) + jnp.einsum(
        "bx,nxy->nby", sin_tab, g_re, precision=precise
    )
    out_re = (
        jnp.einsum("nby,cy->nbc", mid_re, cos_tab, precision=precise)
        - jnp.einsum("nby,cy->nbc", mid_im, sin_tab, precision=precise)
    ) * scale
    out_im = (
        jnp.einsum("nby,cy->nbc", mid_re, sin_tab, precision=precise)
        + jnp.einsum("nby,cy->nbc", mid_im, cos_tab, precision=precise)
    ) * scale
    return (out_re, out_im)


def on_device(
    tile_mask, master_mask, target, inst_master, inst_shift, kernels, kernel_weight, corner_dose
):
    cos_tab, sin_tab = band_tables()
    scale = 1.0 / (P_SIZE * P_SIZE)
    local_tiles = tile_mask.shape[0]
    tile_re, tile_im = spectra(tile_mask.astype(jnp.float32), cos_tab, sin_tab)
    ph_re, ph_im = phase_ramp(inst_shift)

    def picker(count):
        index = jnp.arange(count, dtype=jnp.int32)
        return (inst_master[:, None] == index[None, :]).astype(jnp.float32)

    piece = lax.all_gather(master_mask, "tile", axis=0, tiled=True)
    chosen = picker(piece.shape[0])
    placed = jnp.einsum("tr,rxy->txy", chosen, piece.astype(jnp.float32), precision=precise)
    sel_re, sel_im = spectra(placed, cos_tab, sin_tab)
    spec_re = tile_re + (ph_re * sel_re - ph_im * sel_im)
    spec_im = tile_im + (ph_re * sel_im + ph_im * sel_re)
    goal = target.astype(jnp.float32)
    dose = corner_dose[0]
    kern_count = lax.axis_size("kern")
    kern_pos = lax.axis_index("kern")
    per_dev = kernels.shape[1] // kern_count
    first = kern_pos * per_dev
    mine_kern = lax.dynamic_slice_in_dim(kernels[0], first, per_dev, 0)
    kern_re = mine_kern[:, 0]
    kern_im = mine_kern[:, 1]
    weights = lax.dynamic_slice_in_dim(kernel_weight[0], first, per_dev, 0)

    def make_field(h_re, h_im):
        x_re = h_re * spec_re - h_im * spec_im
        x_im = h_re * spec_im + h_im * spec_re
        return to_field(x_re, x_im, cos_tab, sin_tab, scale)

    def forward(total, item):
        h_re, h_im, weight = item
        f_re, f_im = make_field(h_re, h_im)
        return (total + weight * (f_re * f_re + f_im * f_im), None)

    partial_light, unused = lax.scan(
        forward, jnp.zeros((local_tiles, P_SIZE, P_SIZE), jnp.float32), (kern_re, kern_im, weights)
    )
    intensity = lax.psum(partial_light, "kern")
    resist = jax.nn.sigmoid(steepness * (dose * intensity - threshold))
    sens = 2.0 * (resist - goal) * resist * (1.0 - resist) * steepness * dose

    def backward(acc, item):
        h_re, h_im, weight = item
        f_re, f_im = make_field(h_re, h_im)
        g_re = 2.0 * weight * sens * f_re
        g_im = 2.0 * weight * sens * f_im
        x_re, x_im = adjoint(g_re, g_im, cos_tab, sin_tab, scale)
        return ((acc[0] + h_re * x_re + h_im * x_im, acc[1] + h_re * x_im - h_im * x_re), None)

    zero = jnp.zeros((local_tiles, B, B), jnp.float32)
    grads, unused = lax.scan(backward, (zero, zero), (kern_re, kern_im, weights))
    partial_grad = jnp.stack([grads[0], grads[1]], axis=1)
    summed = lax.psum(partial_grad, ("corner", "kern"))
    tile_grad = back_pixels(summed[:, 0], summed[:, 1], cos_tab, sin_tab)
    back_re = ph_re * summed[:, 0] + ph_im * summed[:, 1]
    back_im = ph_re * summed[:, 1] - ph_im * summed[:, 0]
    masters_all = lax.axis_size("tile") * master_mask.shape[0]
    owner_pick = picker(masters_all)
    terms = jnp.stack(
        [
            jnp.einsum("tm,tbc->mbc", owner_pick, back_re, precision=precise),
            jnp.einsum("tm,tbc->mbc", owner_pick, back_im, precision=precise),
        ],
        axis=1,
    )
    mine = lax.psum_scatter(terms, "tile", scatter_dimension=0, tiled=True)
    master_grad = back_pixels(mine[:, 0], mine[:, 1], cos_tab, sin_tab)
    return (tile_grad, master_grad)


def solution(mesh):
    return jax.shard_map(
        on_device,
        mesh=mesh,
        in_specs=(
            P(("region", "tile"), None, None),
            P(("region", "tile"), None, None),
            P(("region", "tile"), None, None),
            P(("region", "tile")),
            P(("region", "tile"), None),
            P("corner", None, None, None, None),
            P("corner", None),
            P("corner"),
        ),
        out_specs=(P(("region", "tile"), None, None), P(("region", "tile"), None, None)),
        check_vma=False,
    )
```

profile of v0, /device:TPU:0, one launch (start us, length us, event | category | flops | bytes accessed | tf_op | source)
XLA Modules:
  0.0 199.7 jit_solution(11332372084410168777)
XLA Ops:
  7.2 17.7 %all_gather.3 = bf16[4,256,256]{2,1,0:T(8,128)(2,1)S(1)} all-gather(bf16[1,256,256]{2,1,0:T(8,128)(2,1)} %param.13), channel_id=1, replica_groups=mesh['region'=2,'tile'=4,'corner'=2,'kern'=2] {'tile'}, dimensions={0}, use_global_device_ids=true | all-gather | bytes 655360 | tf_op jit(solution)/shard_map/all_gather | solution.py:106
  32.3 37.9 %while.30 = (s32[]{:T(128)}, f32[2,256,256]{2,1,0:T(8,128)S(1)}, f32[6]{0:T(128)S(1)}, f32[6,32,32]{2,1,0:T(8,128)S(1)}, f32[2,32,32]{1,2,0:T(8,128)S(1)}, /*ind...) while((s32[]{:T(128)}, f32[2,256,256]{2,1,0:T(8,128)S(1)}, ...), condition=%wide.region_1.2_spmd.clone.clone.clone.clone, body=%wide.region_0.1_spmd.clone.clone.clone.clone.sunk | while | flops 228810752 | bytes 4981891 | solution.py:133
  37.0 1.6 fusion.466
  41.2 0.8 fusion.464
  43.3 1.6 fusion.466
  47.5 0.8 fusion.464
  49.7 1.6 fusion.466
  53.9 0.8 fusion.464
  56.0 1.6 fusion.466
  60.2 0.8 fusion.464
  62.3 1.6 fusion.466
  66.5 0.8 fusion.464
  68.6 1.6 fusion.466
  70.3 0.8 copy-done.1
  72.0 19.7 %all-reduce.2.cloned.1.call-done = f32[2,256,256]{2,1,0:T(8,128)} async-done(((f32[2,256,256]{2,1,0:T(8,128)}), f32[2,256,256]{2,1,0:T(8,128)}) %all-reduce.2.cloned.1.call-update) | async-done | bytes 524304 | tf_op jit(solution)/shard_map/psum | solution.py:136
  91.7 1.3 multiply_multiply_fusion
  93.0 61.6 %while.31 = (s32[]{:T(128)}, f32[2,32,32]{2,1,0:T(8,128)S(1)}, f32[2,32,32]{2,1,0:T(8,128)S(1)}, f32[6]{0:T(128)S(1)}, f32[2,256,256]{2,1,0:T(8,128)S(1)}, /*ind...) while((s32[]{:T(128)}, f32[2,32,32]{2,1,0:T(8,128)S(1)}, ...), condition=%wide.region_4.5_spmd.clone.clone.clone.clone, body=%wide.region_3.4_spmd.clone.clone.clone.clone.sunk | while | flops 456050688 | bytes 7833771 | solution.py:149
  96.8 0.8 fusion.502
  99.0 0.8 fusion.499
  107.1 0.8 fusion.502
  109.3 0.8 fusion.499
  119.5 0.8 fusion.499
  127.6 0.8 fusion.502
  129.8 0.8 fusion.499
  137.9 0.8 fusion.502
  140.1 0.8 fusion.499
  150.4 0.8 fusion.499
  154.7 12.2 %psum.15 = f32[2,2,32,32]{3,2,0,1:T(8,128)S(1)} all-reduce(f32[2,2,32,32]{3,2,0,1:T(8,128)S(1)} %pad_maximum_fusion.1), channel_id=1, replica_groups=mesh['region'=2,'tile'=4,'corner'=2,'kern'=2] {'corner','kern'}, use_global_device_ids=true, to_apply=%region_5.6 | all-reduce | flops 4096 | bytes 32768 | tf_op jit(solution)/shard_map/psum | solution.py:151
  170.9 1.6 convolution_add_fusion.6
  172.5 16.2 %reduce-scatter.2.cloned.1.call-done = f32[1,2,32,32]{3,2,1,0:T(8,128)} async-done(((f32[4,2,32,32]{3,2,1,0:T(8,128)}), f32[1,2,32,32]{3,2,1,0:T(8,128)}) %reduce-scatter.2.cloned.1.call-update) | async-done | bytes 8208 | tf_op jit(solution)/shard_map/reduce_scatter | solution.py:164
  188.7 1.1 fusion.250
  191.6 1.3 fusion.189
  (229 shorter events, 86.2 us)
Async XLA Ops:
  7.2 24.4 %copy-start = (f32[1,12,2,32,32]{4,3,2,1,0:T(8,128)S(1)}, f32[1,12,2,32,32]{4,3,2,1,0:T(8,128)}, u32[]{:S(2)}) copy-start(f32[1,12,2,32,32]{4,3,2,1,0:T(8,128)} %param.17) | copy-start | bytes 294916
  7.2 84.5 %all-reduce.2.cloned.1.call-start = ((), (), s32[]{:S(2)}) async-start(), calls=%async_computation.1 | async-start | bytes 1048576 | tf_op jit(solution)/shard_map/psum | solution.py:136
  7.2 17.7 %copy-start.4 = (s32[2]{0:T(128)S(1)}, s32[2]{0:T(128)}, u32[]{:S(2)}) copy-start(s32[2]{0:T(128)} %param.15) | copy-start | bytes 28
  26.7 1.0 copy-start.2
  29.7 0.7 copy-start.5
  31.6 0.7 copy-start.7
  70.3 0.8 copy-start.1
  70.3 21.4 %copy-start.3 = (bf16[2,256,256]{2,1,0:T(8,128)(2,1)S(1)}, bf16[2,256,256]{2,1,0:T(8,128)(2,1)}, u32[]{:S(2)}) copy-start(bf16[2,256,256]{2,1,0:T(8,128)(2,1)} %param.14) | copy-start | bytes 786436
  71.1 117.6 %reduce-scatter.2.cloned.1.call-start = ((), (), s32[]{:S(2)}) async-start(), calls=%async_computation.2 | async-start | bytes 163840 | tf_op jit(solution)/shard_map/reduce_scatter | solution.py:164
  188.7 1.2 copy-start.6
Sparse Core Ops, SparseCore 0:
  71.2 20.4 all-reduce.1
  169.5 19.2 reduce-scatter.1
where the time goes:
time: 200 us
  matrix products  99.7 us (50%)
  waiting for transfers between devices  36 us (18%)
  blocking collectives  29.9 us (15%)
  between operations  15 us (8%)
  local copies, waits for them, and re-layouts  11.7 us (6%)
  loops' own time  5.29 us (3%)
    psum x1, waiting for transfers between devices, on_device(): intensity = lax.psum(partial_light, 'kern')  19.7 us
    all_gather x1, blocking collectives, on_device(): piece = lax.all_gather(master_mask, 'tile', axis=0, tiled=True)  17.7 us
    reduce_scatter x1, waiting for transfers between devices, on_device(): mine = lax.psum_scatter(terms, 'tile', scatter_dimension=0, tiled=True)  16.2 us
    dot_general x12, matrix products, to_field(): jnp.einsum('nxc,cy->nxy', half_im, sin_tab, precision=precise)  14.3 us
    psum x1, blocking collectives, on_device(): summed = lax.psum(partial_grad, ('corner', 'kern'))  12.2 us
    dot_general x12, matrix products, to_field(): jnp.einsum('nxc,cy->nxy', half_re, sin_tab, precision=precise)  9.2 us
    dot_general x12, matrix products, to_field(): jnp.einsum('nxc,cy->nxy', half_im, cos_tab, precision=precise)  9.12 us
    dot_general x12, matrix products, to_field(): jnp.einsum('nxc,cy->nxy', half_re, cos_tab, precision=precise)  9.1 us
  transfers between devices with their start and end apart: 2, of which 2 were waited for; matrix products, arithmetic and copies ran while one was open for 2% of the time, Pallas kernels for 0%

commit v1 on v0

--- a/solution.py
+++ b/solution.py
@@ -133,7 +133,7 @@
     partial_light, unused = lax.scan(
         forward, jnp.zeros((local_tiles, P_SIZE, P_SIZE), jnp.float32), (kern_re, kern_im, weights)
     )
-    intensity = lax.psum(partial_light, "kern")
+    intensity = jnp.sum(lax.all_gather(partial_light, "kern"), axis=0)
     resist = jax.nn.sigmoid(steepness * (dose * intensity - threshold))
     sens = 2.0 * (resist - goal) * resist * (1.0 - resist) * steepness * dose
 

time: 200 us -> 191 us (0.955)
  waiting for transfers between devices: 36 us -> 26.3 us
    psum x1 -> x0, waiting for transfers between devices: 19.7 us -> none  [on_device(): intensity = lax.psum(partial_light, 'kern')]
    all_gather x0 -> x1, waiting for transfers between devices: none -> 10.1 us  [on_device(): intensity = jnp.sum(lax.all_gather(partial_light, 'kern'), axis=0)]
where the time goes in v1:
time: 191 us; the launch traced here: 190 us
  matrix products  99.7 us (52%)
  blocking collectives  29.9 us (16%)
  waiting for transfers between devices  26.3 us (14%)
  between operations  15 us (8%)
  local copies, waits for them, and re-layouts  11.8 us (6%)
  loops' own time  5.29 us (3%)
  other arithmetic  2.06 us (1%)
    all_gather x1, blocking collectives, on_device(): piece = lax.all_gather(master_mask, 'tile', axis=0, tiled=True)  17.7 us
    reduce_scatter x1, waiting for transfers between devices, on_device(): mine = lax.psum_scatter(terms, 'tile', scatter_dimension=0, tiled=True)  16.2 us
    dot_general x12, matrix products, to_field(): jnp.einsum('nxc,cy->nxy', half_im, sin_tab, precision=precise)  14.3 us
    psum x1, blocking collectives, on_device(): summed = lax.psum(partial_grad, ('corner', 'kern'))  12.2 us
    all_gather x1, waiting for transfers between devices, on_device(): intensity = jnp.sum(lax.all_gather(partial_light, 'kern'), axis=0)  10.1 us
    dot_general x12, matrix products, to_field(): jnp.einsum('nxc,cy->nxy', half_re, sin_tab, precision=precise)  9.22 us
    dot_general x12, matrix products, to_field(): jnp.einsum('nxc,cy->nxy', half_im, cos_tab, precision=precise)  9.12 us
    dot_general x12, matrix products, to_field(): jnp.einsum('nxc,cy->nxy', half_re, cos_tab, precision=precise)  9.1 us
  transfers between devices with their start and end apart: 2, of which 2 were waited for; matrix products, arithmetic and copies ran while one was open for 2% of the time, Pallas kernels for 0%

profile of v1, /device:TPU:0, one launch (start us, length us, event | category | flops | bytes accessed | tf_op | source)
XLA Modules:
  0.0 190.3 jit_solution(14073371318549059154)
XLA Ops:
  7.2 17.7 %all_gather.9 = bf16[4,256,256]{2,1,0:T(8,128)(2,1)S(1)} all-gather(bf16[1,256,256]{2,1,0:T(8,128)(2,1)} %param.13), channel_id=1, replica_groups=mesh['region'=2,'tile'=4,'corner'=2,'kern'=2] {'tile'}, dimensions={0}, use_global_device_ids=true | all-gather | bytes 655360 | tf_op jit(solution)/shard_map/all_gather | solution.py:106
  32.3 37.9 %while.30 = (s32[]{:T(128)}, f32[2,256,256]{2,1,0:T(8,128)S(1)}, f32[6]{0:T(128)S(1)}, f32[6,32,32]{2,1,0:T(8,128)S(1)}, f32[2,32,32]{1,2,0:T(8,128)S(1)}, /*ind...) while((s32[]{:T(128)}, f32[2,256,256]{2,1,0:T(8,128)S(1)}, ...), condition=%wide.region_1.2_spmd.clone.clone.clone.clone, body=%wide.region_0.1_spmd.clone.clone.clone.clone.sunk | while | flops 228810752 | bytes 4981891 | solution.py:133
  37.0 1.6 fusion.466
  41.2 0.8 fusion.464
  43.3 1.6 fusion.466
  47.5 0.8 fusion.464
  49.7 1.6 fusion.466
  56.0 1.6 fusion.466
  60.2 0.8 fusion.464
  62.3 1.6 fusion.466
  68.6 1.6 fusion.466
  70.3 0.8 copy-done.1
  72.0 10.1 %all-gather.3.cloned.1.call-done = f32[4,256,256]{2,1,0:T(8,128)} async-done(((f32[2,256,256]{2,1,0:T(8,128)}), f32[4,256,256]{2,1,0:T(8,128)}) %all-gather.3.cloned.1.call-update) | async-done | bytes 1048592 | tf_op jit(solution)/shard_map/all_gather | solution.py:136
  82.0 1.4 reduce_sum.9
  83.7 61.6 %while.31 = (s32[]{:T(128)}, f32[2,32,32]{2,1,0:T(8,128)S(1)}, f32[2,32,32]{2,1,0:T(8,128)S(1)}, f32[6]{0:T(128)S(1)}, f32[2,256,256]{2,1,0:T(8,128)S(1)}, /*ind...) while((s32[]{:T(128)}, f32[2,32,32]{2,1,0:T(8,128)S(1)}, ...), condition=%wide.region_4.5_spmd.clone.clone.clone.clone, body=%wide.region_3.4_spmd.clone.clone.clone.clone.sunk | while | flops 456050688 | bytes 7833771 | solution.py:149
  87.5 0.8 fusion.502
  89.7 0.8 fusion.499
  97.8 0.8 fusion.502
  99.9 0.8 fusion.499
  108.1 0.8 fusion.502
  110.2 0.8 fusion.499
  118.3 0.8 fusion.502
  120.5 0.8 fusion.499
  128.6 0.8 fusion.502
  130.8 0.8 fusion.499
  138.9 0.8 fusion.502
  141.0 0.8 fusion.499
  145.4 12.2 %psum.7 = f32[2,2,32,32]{3,2,0,1:T(8,128)S(1)} all-reduce(f32[2,2,32,32]{3,2,0,1:T(8,128)S(1)} %pad_maximum_fusion.1), channel_id=1, replica_groups=mesh['region'=2,'tile'=4,'corner'=2,'kern'=2] {'corner','kern'}, use_global_device_ids=true, to_apply=%region_5.6 | all-reduce | flops 4096 | bytes 32768 | tf_op jit(solution)/shard_map/psum | solution.py:151
  161.6 1.6 convolution_add_fusion.6
  163.2 16.2 %reduce-scatter.2.cloned.1.call-done = f32[1,2,32,32]{3,2,1,0:T(8,128)} async-done(((f32[4,2,32,32]{3,2,1,0:T(8,128)}), f32[1,2,32,32]{3,2,1,0:T(8,128)}) %reduce-scatter.2.cloned.1.call-update) | async-done | bytes 8208 | tf_op jit(solution)/shard_map/reduce_scatter | solution.py:164
  179.4 1.1 fusion.250
  182.2 1.3 fusion.189
  (230 shorter events, 86.4 us)
Async XLA Ops:
  7.2 24.4 %copy-start = (f32[1,12,2,32,32]{4,3,2,1,0:T(8,128)S(1)}, f32[1,12,2,32,32]{4,3,2,1,0:T(8,128)}, u32[]{:S(2)}) copy-start(f32[1,12,2,32,32]{4,3,2,1,0:T(8,128)} %param.17) | copy-start | bytes 294916
  7.2 74.9 %all-gather.3.cloned.1.call-start = ((), (), s32[]{:S(2)}) async-start(), calls=%async_computation.2 | async-start | bytes 1572864 | tf_op jit(solution)/shard_map/all_gather | solution.py:136
  7.2 17.7 %copy-start.4 = (s32[2]{0:T(128)S(1)}, s32[2]{0:T(128)}, u32[]{:S(2)}) copy-start(s32[2]{0:T(128)} %param.15) | copy-start | bytes 28
  26.7 1.0 copy-start.2
  29.7 0.7 copy-start.5
  31.6 0.7 copy-start.7
  70.3 0.8 copy-start.1
  71.1 108.3 %reduce-scatter.2.cloned.1.call-start = ((), (), s32[]{:S(2)}) async-start(), calls=%async_computation.1 | async-start | bytes 163840 | tf_op jit(solution)/shard_map/reduce_scatter | solution.py:164
  82.0 1.4 copy-start.3
  179.4 1.2 copy-start.6
Sparse Core Ops, SparseCore 0:
  71.2 10.7 all-gather.2
  160.1 19.2 reduce-scatter.1
